TPU v7x, 32 devices: a whole 2x2x4 slice. The times are simulated.
32 devices in a mesh: req: 2 (over x), seq: 16 (over z, y, core).
Axes of the slice: x: 2, y: 2, z: 4, core: 2. Of those that a mesh axis runs over, the one named last changes fastest.
Arguments:
- states: bfloat16 [4, 4, 4544], P(None, 'req', 'seq'), may hold values from -6 to 6
- kv_cache: bfloat16 [4, 8192, 128], P('req', 'seq'), may hold values from -48 to 48, as said below
- lengths: int32 [4], replicated, may hold values from 1 to 8188, as said below
- placement: int32 [4], replicated, may hold values from 0 to 3, each once
- norm_gain: bfloat16 [4544], replicated, may hold values from 0.25 to 1.75
- norm_bias: bfloat16 [4544], replicated, may hold values from -1.5 to 1.5
- w_query: bfloat16 [4544, 4544], P('req', 'seq'), may hold values from -0.09375 to 0.09375
- w_keyval: bfloat16 [4544, 128], P('req'), may hold values from -0.09375 to 0.09375
- w_out: bfloat16 [4544, 4544], P('seq', 'req'), may hold values from -0.09375 to 0.09375
- w_up: bfloat16 [4544, 18176], P('req', 'seq'), may hold values from -0.09375 to 0.09375
- w_down: bfloat16 [18176, 4544], P('seq', 'req'), may hold values from -0.046875 to 0.046875
Outputs:
- new_states: bfloat16 [4, 4, 4544], P(None, 'req', 'seq')
- new_cache: bfloat16 [4, 8192, 128], P('req', 'seq')
Inputs may be any that keep to these rules, and one draw needn't show every extreme that they name: Request r's cache holds its first lengths[r] positions; some request has exactly 8188. `kv_cache`: row i is the cache of request placement[i]; positions at or beyond that request's length hold arbitrary values. `placement`: each request is served by exactly one slot.
All inputs are finite; a program needn't handle non-finite values.
Results may differ from a plain program's by a relative error of at most 0.012.
The roundings to bfloat16 on the way count: a program that leaves them out, or rounds other values in their place, can miss the bound.
Values may be sent and summed in bfloat16 or wider, within the bound.
No kernel may reach another device: no remote copies, remote signals or barrier semaphores. Data moves between devices by JAX's collectives and lax.ppermute only.
A program may use at most 192 MiB of HBM per device.

v0:
```python
import jax
import jax.numpy as jnp
from jax import lax
from jax.sharding import PartitionSpec as P

EPSILON = 1e-05
NEGATIVE = -1e30
ALL = ("req", "seq")


def layer_norm(row_block, norm_gain, norm_bias):
    values = row_block.astype(jnp.float32)
    average = jnp.mean(values, axis=-1, keepdims=True)
    centered = values - average
    spread = jnp.mean(centered * centered, axis=-1, keepdims=True)
    scaled = centered * lax.rsqrt(spread + EPSILON)
    return (scaled * norm_gain.astype(jnp.float32) + norm_bias.astype(jnp.float32)).astype(
        jnp.bfloat16
    )


def rotate(vectors, positions):
    head_width = vectors.shape[-1]
    half_width = head_width // 2
    frequency = 10000.0 ** (-(jnp.arange(half_width, dtype=jnp.float32) * 2.0) / head_width)
    angles = positions.astype(jnp.float32)[:, None] * frequency[None, :]
    cosine = jnp.concatenate([jnp.cos(angles), jnp.cos(angles)], axis=-1)[:, None, :]
    sine_wave = jnp.concatenate([jnp.sin(angles), jnp.sin(angles)], axis=-1)[:, None, :]
    turned = jnp.concatenate([-vectors[..., half_width:], vectors[..., :half_width]], axis=-1)
    return vectors * cosine + turned * sine_wave


def shards(
    states,
    kv_cache,
    lengths,
    placement,
    norm_gain,
    norm_bias,
    w_query,
    w_keyval,
    w_out,
    w_up,
    w_down,
):
    steps = states.shape[0]
    group_rows = kv_cache.shape[0]
    seg_length = kv_cache.shape[1]
    head_width = kv_cache.shape[2] // 2
    model_width = norm_gain.shape[0]
    head_count = model_width // head_width
    slice_width = states.shape[2]
    part_width = w_query.shape[0]
    total = placement.shape[0]
    req_size = total // group_rows
    seq_size = model_width // slice_width
    rows = steps * total
    group_index = lax.axis_index("req")
    shard_index = lax.axis_index("seq")
    own_requests = lax.dynamic_slice_in_dim(placement, group_index * group_rows, group_rows, 0)
    slot_lengths = jnp.take(lengths, own_requests)
    step_offsets = jnp.arange(steps, dtype=jnp.int32)
    positions = slot_lengths[None, :] + step_offsets[:, None]
    every = lax.all_gather(states, ALL, axis=0, tiled=False)
    every = every.reshape(req_size, seq_size, steps, group_rows, slice_width)
    every = every.transpose(2, 0, 3, 1, 4).reshape(steps, total, model_width)
    current_all = jnp.take(every, placement, axis=1)
    normed = layer_norm(current_all.reshape(rows, model_width), norm_gain, norm_bias)
    normed_part = lax.dynamic_slice_in_dim(normed, group_index * part_width, part_width, 1)
    part_query = jnp.dot(normed_part, w_query, preferred_element_type=jnp.float32)
    part_keyval = jnp.dot(normed_part, w_keyval, preferred_element_type=jnp.float32)
    part_up = jnp.dot(normed_part, w_up, preferred_element_type=jnp.float32)
    first = lax.psum(jnp.concatenate([part_query, part_keyval, part_up], axis=1), "req")
    query_raw = first[:, :slice_width].astype(jnp.bfloat16).reshape(steps, total, slice_width)
    keyval = first[:, slice_width : slice_width + 2 * head_width].reshape(
        steps, total, 2 * head_width
    )
    up_part = first[:, slice_width + 2 * head_width :]
    own_query = lax.dynamic_slice_in_dim(query_raw, group_index * group_rows, group_rows, 1)
    query_all = lax.all_gather(own_query, "seq", axis=2, tiled=True)
    flat_positions = positions.reshape(-1)
    query_rows = rotate(
        query_all.astype(jnp.float32).reshape(steps * group_rows, head_count, head_width),
        flat_positions,
    ).astype(jnp.bfloat16)
    own_keyval = lax.dynamic_slice_in_dim(keyval, group_index * group_rows, group_rows, 1)
    own_keyval = own_keyval.reshape(steps * group_rows, 2 * head_width)
    new_key = rotate(own_keyval[:, None, :head_width], flat_positions)[:, 0, :]
    new_entry = jnp.concatenate([new_key, own_keyval[:, head_width:]], axis=-1).astype(jnp.bfloat16)
    new_entry = new_entry.reshape(steps, group_rows, 2 * head_width)
    local_slots = jnp.arange(seg_length, dtype=jnp.int32)
    global_positions = shard_index * seg_length + local_slots
    cache_now = kv_cache
    for step_index in range(steps):
        write_mask = global_positions[None, :] == positions[step_index][:, None]
        cache_now = jnp.where(write_mask[:, :, None], new_entry[step_index][:, None, :], cache_now)
    key_rows = cache_now[:, :, :head_width]
    value_rows = cache_now[:, :, head_width:]
    query_heads = (
        query_rows.reshape(steps, group_rows, head_count, head_width)
        .transpose(1, 0, 2, 3)
        .reshape(group_rows, steps * head_count, head_width)
    )
    scores = jnp.einsum(
        "gqd,gsd->gqs", query_heads, key_rows, preferred_element_type=jnp.float32
    ) * head_width ** (-0.5)
    valid = global_positions[None, None, :] <= positions.T[:, :, None]
    valid = jnp.broadcast_to(
        valid[:, :, None, :], (group_rows, steps, head_count, seg_length)
    ).reshape(group_rows, steps * head_count, seg_length)
    local_peak = jnp.max(jnp.where(valid, scores, NEGATIVE), axis=-1)
    weights = jnp.where(valid, jnp.exp(scores - local_peak[:, :, None]), 0.0)
    local_total = jnp.sum(weights, axis=-1)
    local_weighted = jnp.einsum(
        "gqs,gsd->gqd", weights, value_rows, preferred_element_type=jnp.float32
    )
    peak_buffer = jnp.full((total, steps * head_count), NEGATIVE, jnp.float32)
    peak_buffer = lax.dynamic_update_slice_in_dim(
        peak_buffer, local_peak, group_index * group_rows, 0
    )
    peak = lax.pmax(peak_buffer, ALL)
    own_peak = lax.dynamic_slice_in_dim(peak, group_index * group_rows, group_rows, 0)
    scale = jnp.exp(local_peak - own_peak)
    packed = jnp.concatenate(
        [local_weighted * scale[:, :, None], (local_total * scale)[:, :, None]], axis=-1
    )
    packed_buffer = jnp.zeros((total, steps * head_count, head_width + 1), jnp.float32)
    packed_buffer = lax.dynamic_update_slice_in_dim(
        packed_buffer, packed, group_index * group_rows, 0
    )
    summed = lax.psum(packed_buffer, ALL)
    mixed = summed[:, :, :head_width] / summed[:, :, head_width:]
    mixed = (
        mixed.reshape(total, steps, model_width)
        .transpose(1, 0, 2)
        .reshape(rows, model_width)
        .astype(jnp.bfloat16)
    )
    mixed_part = lax.dynamic_slice_in_dim(mixed, shard_index * slice_width, slice_width, 1)
    hidden = jax.nn.gelu(up_part, approximate=False).astype(jnp.bfloat16)
    partial_sum = jnp.dot(mixed_part, w_out, preferred_element_type=jnp.float32) + jnp.dot(
        hidden, w_down, preferred_element_type=jnp.float32
    )
    out_buffer = jnp.zeros((rows, model_width), jnp.float32)
    out_buffer = lax.dynamic_update_slice_in_dim(
        out_buffer, partial_sum, group_index * part_width, 1
    )
    branch = lax.psum(out_buffer, ALL).reshape(steps, total, model_width)
    inverse = jnp.zeros((total,), jnp.int32).at[placement].set(jnp.arange(total, dtype=jnp.int32))
    own_inverse = lax.dynamic_slice_in_dim(inverse, group_index * group_rows, group_rows, 0)
    own_branch = jnp.take(branch, own_inverse, axis=1)
    own_branch = lax.dynamic_slice_in_dim(own_branch, shard_index * slice_width, slice_width, 2)
    new_states = (states.astype(jnp.float32) + own_branch).astype(jnp.bfloat16)
    return (new_states, cache_now)


def solution(mesh):
    in_specs = (
        P(None, "req", "seq"),
        P("req", "seq", None),
        P(),
        P(),
        P(),
        P(),
        P("req", "seq"),
        P("req", None),
        P("seq", "req"),
        P("req", "seq"),
        P("seq", "req"),
    )
    out_specs = (P(None, "req", "seq"), P("req", "seq", None))
    return jax.shard_map(shards, mesh=mesh, in_specs=in_specs, out_specs=out_specs, check_vma=False)
```

profile of v0, /device:TPU:8, one launch (start us, length us, event | category | flops | bytes accessed | tf_op | source)
XLA Modules:
  0.0 437.4 jit_solution(13402356280962080718)
XLA Ops:
  7.2 0.8 compare_select_fusion.2
  8.0 0.7 compare_and_fusion
  8.6 0.8 dynamic-slice.1
  9.4 0.8 dynamic-slice.2
  10.2 38.8 %all-gather = bf16[128,2,284]{2,1,0:T(2,128)(2,1)S(1)} all-gather(bf16[4,2,284]{2,1,0:T(2,128)(2,1)} %param.11), channel_id=2, replica_groups=mesh['req'=2,'seq'=16] {'req','seq'}, dimensions={0}, use_global_device_ids=true | all-gather | bytes 149952 | tf_op jit(solution)/shard_map/all_gather | solution.py:64
  49.0 0.3 reshape.348
  49.4 0.7 gather_fusion.1
  50.1 0.3 convert_reduce_fusion
  50.4 0.3 fusion.5
  51.3 3.5 fusion.96
  54.8 0.3 fusion.94
  55.1 0.4 fusion.95
  55.5 0.8 concatenate.40
  56.5 0.6 gather_fusion
  57.7 0.1 copy.81
  58.0 0.2 reshape.346
  58.3 19.3 %all-reduce.4.cloned.1.call-done = f32[16,1548]{1,0:T(8,128)} async-done(((f32[16,1548]{1,0:T(8,128)}), f32[16,1548]{1,0:T(8,128)}) %all-reduce.4.cloned.1.call-update) | async-done | bytes 99088 | tf_op jit(solution)/shard_map/psum | solution.py:73
  77.6 0.8 slice.99
  78.4 0.7 slice.124
  79.2 0.2 copy.88
  79.4 32.2 %all_gather.11 = bf16[4,2,4544]{0,1,2:T(2,128)(2,1)} all-gather(bf16[4,2,284]{0,1,2:T(2,128)(2,1)S(1)} %copy.88), channel_id=1, replica_groups=mesh['req'=2,'seq'=16] {'seq'}, dimensions={2}, use_global_device_ids=true | all-gather | bytes 77248 | tf_op jit(solution)/shard_map/all_gather | solution.py:80
  111.6 5.2 %copy.73 = bf16[4,2,4544]{2,0,1:T(4,128)(2,1)S(1)} copy(bf16[4,2,4544]{0,1,2:T(2,128)(2,1)} %all_gather.11) | data formatting | bytes 145408 | tf_op jit(solution)/shard_map/all_gather | solution.py:80
  116.8 0.2 reshape.351
  117.1 0.2 reshape.350
  117.9 0.2 copy.78
  118.1 0.2 fusion.8
  118.2 0.2 copy.80
  118.5 0.2 select_select_fusion
  118.8 0.5 select_reduce_fusion
  119.3 41.3 %pmax.7 = f32[4,284]{1,0:T(4,128)S(1)} all-reduce(f32[4,284]{1,0:T(4,128)S(1)} %constant_dynamic-update-slice_fusion.1), channel_id=1, replica_groups=mesh['req'=2,'seq'=16] {'req','seq'}, use_global_device_ids=true, to_apply=%region_5.6 | all-reduce | flops 1136 | bytes 9088 | tf_op jit(solution)/shard_map/pmax | solution.py:121
  160.6 0.4 fusion
  161.0 0.4 convolution_multiply_fusion.1
  161.5 0.2 copy.82
  161.7 0.8 copy-done.2
  162.6 0.6 scatter_custom_fusion
  163.2 129.3 %all-reduce.6.cloned.1.call-done = f32[4,284,65]{2,1,0:T(8,128)} async-done(((f32[4,284,65]{2,1,0:T(8,128)}), f32[4,284,65]{2,1,0:T(8,128)}) %all-reduce.6.cloned.1.call-update) | async-done | bytes 295376 | tf_op jit(solution)/shard_map/psum | solution.py:131
  292.5 1.5 slice_reduce_fusion
  294.0 1.3 fusion.1
  295.3 0.2 convert_element_type.69
  295.6 0.4 fusion.55
  296.0 0.2 copy-done.6
  296.2 3.4 convolution_add_fusion
  299.7 1.3 dynamic_update_slice.11
  301.1 0.8 copy.84
  302.0 0.8 copy.86
  302.9 125.7 %all-reduce.8.cloned.1.call-done = f32[4,4,4544]{2,0,1:T(4,128)} async-done(((f32[4,4,4544]{2,0,1:T(4,128)}), f32[4,4,4544]{2,0,1:T(4,128)}) %all-reduce.8.cloned.1.call-update) | async-done | bytes 290832 | tf_op jit(solution)/shard_map/psum | solution.py:148
  428.5 1.6 gather_fusion.2
  430.2 0.6 copy.85
  (81 shorter events, 3.2 us)
Async XLA Ops:
  7.2 288.4 %copy-start = (bf16[284,2272]{1,0:T(8,128)(2,1)S(1)}, bf16[284,2272]{1,0:T(8,128)(2,1)}, u32[]{:S(2)}) copy-start(bf16[284,2272]{1,0:T(8,128)(2,1)} %param.19) | copy-start | bytes 3871492
  7.2 70.4 %all-reduce.4.cloned.1.call-start = ((), (), s32[]{:S(2)}) async-start(), calls=%async_computation | async-start | bytes 212992 | tf_op jit(solution)/shard_map/psum | solution.py:73
  51.3 3.5 copy-start.4
  51.3 3.8 copy-start.3
  54.8 1.6 copy-start.8
  54.8 1.7 copy-start.1
  55.1 2.6 copy-start.5
  56.3 236.2 %all-reduce.6.cloned.1.call-start = ((), (), s32[]{:S(2)}) async-start(), calls=%async_computation.1 | async-start | bytes 1179648 | tf_op jit(solution)/shard_map/psum | solution.py:131
  161.7 0.8 copy-start.2
  162.6 266.0 %all-reduce.8.cloned.1.call-start = ((), (), s32[]{:S(2)}) async-start(), calls=%async_computation.2 | async-start | bytes 589824 | tf_op jit(solution)/shard_map/psum | solution.py:148
  295.3 0.9 copy-start.6
  301.0 129.2 %copy-start.7 = (bf16[4,2,284]{2,1,0:T(2,128)(2,1)S(1)}, bf16[4,2,284]{2,1,0:T(2,128)(2,1)}, u32[]{:S(2)}) copy-start(bf16[4,2,284]{2,1,0:T(2,128)(2,1)} %param.11) | copy-start | bytes 13636
Sparse Core Ops, SparseCore 0:
  56.4 21.1 all-reduce.3
  162.7 129.7 all-reduce.5
  302.1 126.4 all-reduce.7
where the time goes:
time: 438 us; the launch traced here: 437 us
  waiting for transfers between devices  274 us (63%)
  blocking collectives  112 us (26%)
  local copies, waits for them, and re-layouts  22.3 us (5%)
  between operations  14.2 us (3%)
  matrix products  8.89 us (2%)
  other arithmetic  5.32 us (1%)
    psum x1, waiting for transfers between devices, shards(): summed = lax.psum(packed_buffer, ALL)  129 us
    psum x1, waiting for transfers between devices, shards(): branch = lax.psum(out_buffer, ALL).reshape(steps, total, model_width)  126 us
    pmax x1, blocking collectives, shards(): peak = lax.pmax(peak_buffer, ALL)  41.3 us
    all_gather x1, blocking collectives, shards(): every = lax.all_gather(states, ALL, axis=0, tiled=False)  38.8 us
    all_gather x1, blocking collectives, shards(): query_all = lax.all_gather(own_query, 'seq', axis=2, tiled=True)  32.2 us
    psum x1, waiting for transfers between devices, shards(): lax.psum(jnp.concatenate([part_query, part_keyval, part_up], axis=1), 'req')  19.3 us
  transfers between devices with their start and end apart: 3, of which 3 were waited for; matrix products, arithmetic and copies ran while one was open for 1% of the time, Pallas kernels for 0%

commit v1 on v0

--- a/solution.py
+++ b/solution.py
@@ -145,7 +145,9 @@
     out_buffer = lax.dynamic_update_slice_in_dim(
         out_buffer, partial_sum, group_index * part_width, 1
     )
-    branch = lax.psum(out_buffer, ALL).reshape(steps, total, model_width)
+    branch = lax.psum(lax.psum(out_buffer, axis_name="seq"), axis_name="req").reshape(
+        steps, total, model_width
+    )
     inverse = jnp.zeros((total,), jnp.int32).at[placement].set(jnp.arange(total, dtype=jnp.int32))
     own_inverse = lax.dynamic_slice_in_dim(inverse, group_index * group_rows, group_rows, 0)
     own_branch = jnp.take(branch, own_inverse, axis=1)

time: 438 us -> 427 us (0.975)
  waiting for transfers between devices: 274 us -> 260 us
    psum x1 -> x2, waiting for transfers between devices: 126 us -> 111 us  [the longest x1 89.2 us: shards(): lax.psum(out_buffer, axis_name='seq')]
  transfers between devices with their start and end apart: 3 -> 4, of which waited for: 3 -> 4; matrix products, arithmetic and copies ran while one was open for 1% -> 1% of each run, Pallas kernels for 0% -> 0%
where the time goes in v1:
time: 427 us; the launch traced here: 425 us
  waiting for transfers between devices  260 us (61%)
  blocking collectives  112 us (26%)
  local copies, waits for them, and re-layouts  24 us (6%)
  between operations  14.2 us (3%)
  matrix products  8.89 us (2%)
  other arithmetic  5.32 us (1%)
    psum x1, waiting for transfers between devices, shards(): summed = lax.psum(packed_buffer, ALL)  130 us
    psum x1, waiting for transfers between devices, shards(): lax.psum(out_buffer, axis_name='seq')  89.2 us
    pmax x1, blocking collectives, shards(): peak = lax.pmax(peak_buffer, ALL)  41.3 us
    all_gather x1, blocking collectives, shards(): every = lax.all_gather(states, ALL, axis=0, tiled=False)  38.8 us
    all_gather x1, blocking collectives, shards(): query_all = lax.all_gather(own_query, 'seq', axis=2, tiled=True)  32.2 us
    psum x1, waiting for transfers between devices, shards(): lax.psum(lax.psum(out_buffer, axis_name='seq'), axis_name='req')  21.5 us
    psum x1, waiting for transfers between devices, shards(): lax.psum(jnp.concatenate([part_query, part_keyval, part_up], axis=1), 'req')  19.3 us
  transfers between devices with their start and end apart: 4, of which 4 were waited for; matrix products, arithmetic and copies ran while one was open for 1% of the time, Pallas kernels for 0%

profile of v1, /device:TPU:8, one launch (start us, length us, event | category | flops | bytes accessed | tf_op | source)
XLA Modules:
  0.0 424.8 jit_solution(7119558214725713767)
XLA Ops:
  7.2 0.8 compare_select_fusion.2
  8.0 0.7 compare_and_fusion
  8.6 0.8 dynamic-slice.1
  9.4 0.8 dynamic-slice.2
  10.2 38.8 %all-gather = bf16[128,2,284]{2,1,0:T(2,128)(2,1)S(1)} all-gather(bf16[4,2,284]{2,1,0:T(2,128)(2,1)} %param.11), channel_id=2, replica_groups=mesh['req'=2,'seq'=16] {'req','seq'}, dimensions={0}, use_global_device_ids=true | all-gather | bytes 149952 | tf_op jit(solution)/shard_map/all_gather | solution.py:64
  49.0 0.3 reshape.348
  49.4 0.7 gather_fusion.1
  50.1 0.3 convert_reduce_fusion
  50.4 0.3 fusion.5
  51.3 3.5 fusion.96
  54.8 0.3 fusion.94
  55.1 0.4 fusion.95
  55.5 0.8 concatenate.40
  56.5 0.6 gather_fusion
  58.0 0.2 reshape.346
  58.3 19.3 %all-reduce.5.cloned.1.call-done = f32[16,1548]{1,0:T(8,128)} async-done(((f32[16,1548]{1,0:T(8,128)}), f32[16,1548]{1,0:T(8,128)}) %all-reduce.5.cloned.1.call-update) | async-done | bytes 99088 | tf_op jit(solution)/shard_map/psum | solution.py:73
  77.6 0.8 slice.99
  78.4 0.7 slice.124
  79.2 0.2 copy.88
  79.4 32.2 %all_gather.11 = bf16[4,2,4544]{0,1,2:T(2,128)(2,1)} all-gather(bf16[4,2,284]{0,1,2:T(2,128)(2,1)S(1)} %copy.88), channel_id=1, replica_groups=mesh['req'=2,'seq'=16] {'seq'}, dimensions={2}, use_global_device_ids=true | all-gather | bytes 77248 | tf_op jit(solution)/shard_map/all_gather | solution.py:80
  111.6 5.2 %copy.73 = bf16[4,2,4544]{2,0,1:T(4,128)(2,1)S(1)} copy(bf16[4,2,4544]{0,1,2:T(2,128)(2,1)} %all_gather.11) | data formatting | bytes 145408 | tf_op jit(solution)/shard_map/all_gather | solution.py:80
  116.8 0.2 reshape.351
  117.1 0.2 reshape.350
  117.9 0.2 copy.78
  118.2 0.2 copy.80
  118.5 0.2 select_select_fusion
  118.8 0.5 select_reduce_fusion
  119.3 41.3 %pmax.7 = f32[4,284]{1,0:T(4,128)S(1)} all-reduce(f32[4,284]{1,0:T(4,128)S(1)} %constant_dynamic-update-slice_fusion.1), channel_id=1, replica_groups=mesh['req'=2,'seq'=16] {'req','seq'}, use_global_device_ids=true, to_apply=%region_5.6 | all-reduce | flops 1136 | bytes 9088 | tf_op jit(solution)/shard_map/pmax | solution.py:121
  160.6 0.4 fusion
  161.0 0.4 convolution_multiply_fusion.1
  161.7 0.8 copy-done.2
  162.6 129.9 %all-reduce.7.cloned.1.call-done = f32[4,284,65]{2,1,0:T(8,128)} async-done(((f32[4,284,65]{2,1,0:T(8,128)}), f32[4,284,65]{2,1,0:T(8,128)}) %all-reduce.7.cloned.1.call-update) | async-done | bytes 295376 | tf_op jit(solution)/shard_map/psum | solution.py:131
  292.5 1.5 slice_reduce_fusion
  294.0 1.3 fusion.1
  295.3 0.2 convert_element_type.69
  295.6 0.4 fusion.55
  296.0 0.2 copy-done.7
  296.2 3.4 convolution_add_fusion
  299.7 1.3 dynamic_update_slice.11
  301.0 0.7 copy-done.4
  301.8 89.2 %all-reduce.9.cloned.1.call-done = f32[16,4544]{1,0:T(8,128)} async-done(((f32[16,4544]{1,0:T(8,128)}), f32[16,4544]{1,0:T(8,128)}) %all-reduce.9.cloned.1.call-update) | async-done | bytes 290832 | tf_op jit(solution)/shard_map/psum | solution.py:148
  391.0 1.0 reshape.355
  392.1 0.8 copy.84
  392.9 0.6 scatter_custom_fusion
  393.6 0.8 copy.86
  394.4 21.5 %all-reduce.11.cloned.1.call-done = f32[4,4,4544]{2,0,1:T(4,128)} async-done(((f32[4,4,4544]{2,0,1:T(4,128)}), f32[4,4,4544]{2,0,1:T(4,128)}) %all-reduce.11.cloned.1.call-update) | async-done | bytes 290832 | tf_op jit(solution)/shard_map/psum | solution.py:148
  416.0 1.6 gather_fusion.2
  417.7 0.6 copy.85
  (86 shorter events, 3.7 us)
Async XLA Ops:
  7.2 288.5 %copy-start = (bf16[284,2272]{1,0:T(8,128)(2,1)S(1)}, bf16[284,2272]{1,0:T(8,128)(2,1)}, u32[]{:S(2)}) copy-start(bf16[284,2272]{1,0:T(8,128)(2,1)} %param.19) | copy-start | bytes 3871492
  7.2 70.4 %all-reduce.5.cloned.1.call-start = ((), (), s32[]{:S(2)}) async-start(), calls=%async_computation | async-start | bytes 212992 | tf_op jit(solution)/shard_map/psum | solution.py:73
  51.3 3.5 copy-start.5
  51.3 3.8 copy-start.3
  54.8 1.6 copy-start.9
  54.8 1.7 copy-start.1
  55.1 2.6 copy-start.6
  56.3 236.2 %all-reduce.7.cloned.1.call-start = ((), (), s32[]{:S(2)}) async-start(), calls=%async_computation.1 | async-start | bytes 1179648 | tf_op jit(solution)/shard_map/psum | solution.py:131
  161.7 0.8 copy-start.2
  162.6 228.4 %all-reduce.9.cloned.1.call-start = ((), (), s32[]{:S(2)}) async-start(), calls=%async_computation.2 | async-start | bytes 589824 | tf_op jit(solution)/shard_map/psum | solution.py:148
  295.3 0.9 copy-start.7
  301.0 0.7 copy-start.4
  301.7 115.8 %copy-start.8 = (bf16[4,2,284]{2,1,0:T(2,128)(2,1)S(1)}, bf16[4,2,284]{2,1,0:T(2,128)(2,1)}, u32[]{:S(2)}) copy-start(bf16[4,2,284]{2,1,0:T(2,128)(2,1)} %param.11) | copy-start | bytes 13636
  301.7 114.2 %all-reduce.11.cloned.1.call-start = ((), (), s32[]{:S(2)}) async-start(), calls=%async_computation.3 | async-start | bytes 589824 | tf_op jit(solution)/shard_map/psum | solution.py:148
Sparse Core Ops, SparseCore 0:
  56.4 21.1 all-reduce.4
  162.7 129.7 all-reduce.6
  301.9 89.1 all-reduce.8
  393.2 22.6 all-reduce.10
